TPU v7x, 256 devices: a whole 4x4x8 slice. The times are simulated.
256 devices in a mesh: row: 16 (over x, z_hi, core), col: 4 (over y), rep: 4 (over z_lo).
Axes of the slice: x: 4, y: 4, z: 8 (z_hi: 2, z_lo: 4; z = z_hi * 4 + z_lo), core: 2. Of those that a mesh axis runs over, the one named last changes fastest.
Arguments:
- integrals: bfloat16 [8, 32, 60, 128, 128], P(None, 'row', 'rep', 'col'), may hold values from -0.0625 to 0.0625
- amplitudes: bfloat16 [8, 16, 60, 128, 128], P(None, 'col', 'rep', 'row'), may hold values from -6 to 6
- virt_count: int32 [8], replicated, may hold values from 76 to 128, as said below
- occ_irrep: int32 [60], replicated, may hold values from 0 to 7
Outputs:
- cycle: bfloat16 [8, 32, 128, 16, 128], P('rep', 'row', None, 'col')
Inputs may be any that keep to these rules, and one draw needn't show every extreme that they name: `virt_count`: one irrep has exactly 128 virtual orbitals.
All inputs are finite; a program needn't handle non-finite values.
Results may differ from a plain program's by a relative error of at most 0.001.
Values may be sent and summed in bfloat16 or wider, within the bound.
No kernel may reach another device: no remote copies, remote signals or barrier semaphores. Data moves between devices by JAX's collectives and lax.ppermute only.
A program may use at most 128 MiB of HBM per device.

v0:
```python
import jax
import jax.numpy as jnp
from jax import lax
from jax.sharding import PartitionSpec as P


def contract(w_part, t_part):
    w_full = lax.all_gather(w_part, "col", axis=3, tiled=True)
    return jnp.einsum(
        "gikca,gjkcb->giajb",
        w_full,
        lax.all_gather(t_part, "row", axis=3, tiled=True),
        preferred_element_type=jnp.float32,
    )


def body(integrals, amplitudes, virt_count, occ_irrep):
    ngroup = integrals.shape[0]
    k_local = integrals.shape[2]
    c_local = integrals.shape[3]
    nvirt = integrals.shape[4]
    rep_index = lax.axis_index("rep")
    col_index = lax.axis_index("col")
    occ_local = lax.dynamic_slice_in_dim(occ_irrep, rep_index * k_local, k_local)
    groups = jnp.arange(ngroup, dtype=jnp.int32)
    blocks = jnp.bitwise_xor(groups[:, None], occ_local[None, :])
    onehot = blocks[:, :, None] == groups[None, None, :]
    limit = jnp.sum(jnp.where(onehot, virt_count[None, None, :], 0), axis=2)
    c_global = col_index * c_local + jnp.arange(c_local, dtype=jnp.int32)
    c_live = c_global[None, None, :] < limit[:, :, None]
    places = jnp.arange(nvirt, dtype=jnp.int32)
    a_live = places[None, :] < virt_count[:, None]
    keep = c_live[:, None, :, :, None] & a_live[:, None, None, None, :]
    masked = jnp.where(keep, integrals, jnp.zeros_like(integrals))
    owned = ngroup // lax.axis_size("rep")
    partial_cycle = contract(masked, amplitudes)
    summed = lax.psum_scatter(partial_cycle, "rep", scatter_dimension=0, tiled=True)
    own_counts = lax.dynamic_slice_in_dim(virt_count, rep_index * owned, owned)
    b_live = places[None, :] < own_counts[:, None]
    result = jnp.where(b_live[:, None, None, None, :], summed, jnp.zeros_like(summed))
    return result.astype(jnp.bfloat16)


def solution(mesh):
    return jax.shard_map(
        body,
        mesh=mesh,
        in_specs=(P(None, "row", "rep", "col", None), P(None, "col", "rep", "row", None), P(), P()),
        out_specs=P("rep", "row", None, "col", None),
        check_vma=False,
    )
```

profile of v0, /device:TPU:1, one launch (start us, length us, event | category | flops | bytes accessed | tf_op | source)
XLA Modules:
  0.0 377.3 jit_solution(17503319874373990578)
XLA Ops:
  6.5 0.0 all-gather.3.cloned.1.call-start
  6.5 0.7 iota_compare_fusion.1
  7.3 0.7 dynamic_slice.7
  8.0 0.7 select_reduce_fusion
  8.7 0.1 broadcast_compare_fusion
  8.8 0.8 broadcast_and_fusion
  9.6 3.1 broadcast_select_fusion
  12.7 0.0 all-gather.3.cloned.1.call-update
  12.8 0.0 all-gather.5.cloned.1.call-start
  12.8 0.7 all-gather.5.cloned.1.call-update
  13.5 0.0 copy-start
  13.5 0.0 reduce-scatter.2.cloned.1.call-start
  13.6 84.3 %all-gather.3.cloned.1.call-done = bf16[8,2,15,128,128]{4,3,2,1,0:T(8,128)(2,1)} async-done(((bf16[8,2,15,32,128]{4,3,2,1,0:T(8,128)(2,1)}), bf16[8,2,15,128,128]{4,3,2,1,0:T(8,128)(2,1)}) %all-gather.3.cloned.1.call-update) | async-done | bytes 7864336 | tf_op jit(solution)/shard_map/all_gather | solution.py:8
  97.8 179.9 %all-gather.5.cloned.1.call-done = bf16[8,4,15,128,128]{4,3,2,1,0:T(8,128)(2,1)} async-done(((bf16[8,4,15,8,128]{4,3,2,1,0:T(8,128)(2,1)}), bf16[8,4,15,128,128]{4,3,2,1,0:T(8,128)(2,1)}) %all-gather.5.cloned.1.call-update) | async-done | bytes 15728656 | tf_op jit(solution)/shard_map/all_gather | solution.py:12
  277.7 14.3 %fusion.3 = f32[8,2,128,4,128]{4,2,3,1,0:T(8,128)} fusion(bf16[8,4,15,128,128]{4,3,2,1,0:T(8,128)(2,1)} %all-gather.5.cloned.1.call-done, bf16[8,2,15,128,128]{4,3,2,1,0:T(8,128)(2,1)} %all-gather.3.cloned.1.call-done), kind=kOutput, calls=%fused_computation.3 | convolution fusion | flops 4026531840 | bytes 27787264 | tf_op jit(solution)/shard_map/gikca,gjkcb->giajb/dot_general | solution.py:9
  292.0 0.0 reduce-scatter.2.cloned.1.call-update
  292.1 0.0 copy-done
  292.1 0.1 dynamic_slice.6
  292.2 0.1 iota_compare_fusion.2
  292.2 76.0 %reduce-scatter.2.cloned.1.call-done = f32[2,2,128,4,128]{4,2,3,1,0:T(8,128)} async-done(((f32[8,2,128,4,128]{4,2,3,1,0:T(8,128)}), f32[2,2,128,4,128]{4,2,3,1,0:T(8,128)}) %reduce-scatter.2.cloned.1.call-update) | async-done | bytes 1048592 | tf_op jit(solution)/shard_map/reduce_scatter | solution.py:37
  368.2 1.3 select_convert_fusion
  369.6 1.2 copy.6
  (2 shorter events, 0.0 us)
Async XLA Ops:
  6.5 91.3 %all-gather.3.cloned.1.call-start = ((), (), s32[]{:S(2)}) async-start(), calls=%async_computation.1 | async-start | bytes 9830400 | tf_op jit(solution)/shard_map/all_gather | solution.py:8
  12.8 265.0 %all-gather.5.cloned.1.call-start = ((), (), s32[]{:S(2)}) async-start(), calls=%async_computation.2 | async-start | bytes 16711680 | tf_op jit(solution)/shard_map/all_gather | solution.py:12
  13.5 278.6 %copy-start = (s32[8]{0:T(128)S(1)}, s32[8]{0:T(128)}, u32[]{:S(2)}) copy-start(s32[8]{0:T(128)} %param.6) | copy-start | bytes 100
  13.5 354.7 %reduce-scatter.2.cloned.1.call-start = ((), (), s32[]{:S(2)}) async-start(), calls=%async_computation.3 | async-start | bytes 5242880 | tf_op jit(solution)/shard_map/reduce_scatter | solution.py:37
Sparse Core Ops, SparseCore 0:
  12.9 84.8 all-gather.2
  100.4 177.3 all-gather.4
  292.2 75.9 reduce-scatter.1
where the time goes:
time: 377 us
  waiting for transfers between devices  341 us (90%)
  matrix products  14.3 us (4%)
  between operations  13.2 us (4%)
  other arithmetic  6.86 us (2%)
    all_gather x1, waiting for transfers between devices, contract(): lax.all_gather(t_part, 'row', axis=3, tiled=True)  180 us
    all_gather x1, waiting for transfers between devices, contract(): w_full = lax.all_gather(w_part, 'col', axis=3, tiled=True)  84.3 us
    reduce_scatter x1, waiting for transfers between devices, body(): lax.psum_scatter(partial_cycle, 'rep', scatter_dimension=0, tiled=True)  76 us
    dot_general x1, matrix products, contract(): jnp.einsum('gikca,gjkcb->giajb', w_full, lax.all_gather(t_part, 'row', ax...  14.3 us
  transfers between devices with their start and end apart: 3, of which 3 were waited for; matrix products, arithmetic and copies ran while one was open for 0% of the time, Pallas kernels for 0%

commit v1 on v0

--- a/solution.py
+++ b/solution.py
@@ -5,7 +5,23 @@
 
 
 def contract(w_part, t_part):
-    w_full = lax.all_gather(w_part, "col", axis=3, tiled=True)
+    out_arr, v_next, state_now = (lax.psum(1, "col"), lax.axis_index("col"), w_part.shape[3])
+    runs = [(m, (m + 1) % out_arr) for m in range(out_arr)]
+    by_place = [(m, (m - 1) % out_arr) for m in range(out_arr)]
+    w_full = jnp.zeros((*w_part.shape[:3], out_arr * state_now, *w_part.shape[4:]), w_part.dtype)
+    w_full = lax.dynamic_update_slice_in_dim(w_full, w_part, v_next * state_now, axis=3)
+    r1 = arr_now = w_part
+    current_block = out_arr // 2
+    for dev in range(1, current_block + 1):
+        r1 = lax.ppermute(r1, "col", runs)
+        w_full = lax.dynamic_update_slice_in_dim(
+            w_full, r1, (v_next - dev) % out_arr * state_now, axis=3
+        )
+        if dev < out_arr - current_block:
+            arr_now = lax.ppermute(arr_now, "col", by_place)
+            w_full = lax.dynamic_update_slice_in_dim(
+                w_full, arr_now, (v_next + dev) % out_arr * state_now, axis=3
+            )
     return jnp.einsum(
         "gikca,gjkcb->giajb",
         w_full,

time: 377 us -> 583 us (1.55); the launches traced: 377 us -> 572 us
  local copies, waits for them, and re-layouts: 2.01 us -> 409 us
  waiting for transfers between devices: 341 us -> 128 us
    dynamic_update_slice x0 -> x4, local copies, waits for them, and re-layouts: none -> 372 us  [the longest x2 198 us: contract(): lax.dynamic_update_slice_in_dim(w_full, r1, (v_next - dev) % out_arr * st...]
    all_gather x1, waiting for transfers between devices: 180 us -> 0.01 us  [contract(): lax.all_gather(t_part, 'row', axis=3, tiled=True)]
    all_gather x1 -> x0, waiting for transfers between devices: 84.3 us -> none  [contract(): w_full = lax.all_gather(w_part, 'col', axis=3, tiled=True)]
    ppermute x0 -> x3, waiting for transfers between devices: none -> 40.6 us  [the longest x2 40.6 us: contract(): r1 = lax.ppermute(r1, 'col', runs)]
    ppermute x0 -> x3, local copies, waits for them, and re-layouts: none -> 23.8 us  [the longest x2 15.8 us: contract(): r1 = lax.ppermute(r1, 'col', runs)]
    reduce_scatter x1, waiting for transfers between devices: 76 us -> 86.4 us  [body(): lax.psum_scatter(partial_cycle, 'rep', scatter_dimension=0, tiled=True)]
  transfers between devices with their start and end apart: 3 -> 5, of which waited for: 3 -> 2; matrix products, arithmetic and copies ran while one was open for 0% -> 72% of each run, Pallas kernels for 0% -> 0%
where the time goes in v1:
time: 583 us; the launch traced here: 572 us
  local copies, waits for them, and re-layouts  409 us (70%)
  waiting for transfers between devices  128 us (22%)
  between operations  13.5 us (2%)
  matrix products  11.5 us (2%)
    dynamic_update_slice x2, local copies, waits for them, and re-layouts, contract(): lax.dynamic_update_slice_in_dim(w_full, r1, (v_next - dev) % out_arr * st...  198 us
    dynamic_update_slice x1, local copies, waits for them, and re-layouts, contract(): lax.dynamic_update_slice_in_dim(w_full, arr_now, (v_next + dev) % out_arr...  98.7 us
    reduce_scatter x1, waiting for transfers between devices, body(): lax.psum_scatter(partial_cycle, 'rep', scatter_dimension=0, tiled=True)  86.4 us
    dynamic_update_slice x1, local copies, waits for them, and re-layouts, contract(): lax.dynamic_update_slice_in_dim(w_full, w_part, v_next * state_now, axis=3)  75.9 us
    ppermute x2, waiting for transfers between devices, contract(): r1 = lax.ppermute(r1, 'col', runs)  40.6 us
    ppermute x2, local copies, waits for them, and re-layouts, contract(): r1 = lax.ppermute(r1, 'col', runs)  15.8 us
  transfers between devices with their start and end apart: 5, of which 2 were waited for; matrix products, arithmetic and copies ran while one was open for 72% of the time, Pallas kernels for 0%

profile of v1, /device:TPU:1, one launch (start us, length us, event | category | flops | bytes accessed | tf_op | source)
XLA Modules:
  0.0 572.4 jit_solution(15484800934928311996)
XLA Ops:
  6.5 0.0 all-gather.2.cloned.1.call-start
  6.5 0.7 all-gather.2.cloned.1.call-update
  7.3 0.0 reduce-scatter.2.cloned.1.call-start
  7.3 0.7 dynamic_slice.7
  8.0 0.7 select_reduce_fusion
  8.8 0.7 iota_compare_fusion.1
  9.5 0.1 broadcast_compare_fusion
  9.6 0.8 broadcast_and_fusion
  10.4 1.7 broadcast_select_fusion
  12.1 2.2 collective-permute-start
  14.3 1.5 collective-permute-start.1
  15.9 40.6 %collective-permute-done = bf16[8,2,15,32,128]{4,3,2,1,0:T(8,128)(2,1)} collective-permute-done((bf16[8,2,15,32,128]{4,3,2,1,0:T(8,128)(2,1)S(1)}, bf16[8,2,15,32,128]{4,3,2,1,0:T(8,128)(2,1)}, u32[]{:S(2)}, u32[]{:S(2)}) %collective-permute-start) | collective-permute-done | bytes 1966112 | tf_op jit(solution)/shard_map/ppermute | solution.py:16
  56.5 1.5 collective-permute-start.2
  58.0 5.7 copy.10
  63.7 5.2 broadcast_in_dim.32
  68.9 75.9 %dynamic_update_slice.12 = bf16[8,2,15,128,128]{3,4,2,1,0:T(8,128)(2,1)} dynamic-update-slice(bf16[8,2,15,128,128]{3,4,2,1,0:T(8,128)(2,1)} %broadcast_in_dim.32, bf16[8,2,15,32,128]{3,4,2,1,0:T(8,128)(2,1)} %copy.10, s32[]{:T(128)} %constant.38.clone.1, s32[]{:T(128)} %constant.38.clone.1, s32[]{:T(128)} %constant.38.clone.1, s32[]{:T(128)S(6)} %select_n.49, s32[]{:T(128)} %constant.38.clone.1) | dynamic-update-slice | bytes 3932164 | tf_op jit(solution)/shard_map/dynamic_update_slice | solution.py:12
  144.8 7.9 %copy.11 = bf16[8,2,15,32,128]{3,4,2,1,0:T(8,128)(2,1)} copy(bf16[8,2,15,32,128]{4,3,2,1,0:T(8,128)(2,1)} %collective-permute-done) | data formatting | bytes 3932160 | tf_op jit(solution)/shard_map/ppermute | solution.py:16
  152.7 98.8 %dynamic_update_slice.13 = bf16[8,2,15,128,128]{3,4,2,1,0:T(8,128)(2,1)} dynamic-update-slice(bf16[8,2,15,128,128]{3,4,2,1,0:T(8,128)(2,1)} %dynamic_update_slice.12, bf16[8,2,15,32,128]{3,4,2,1,0:T(8,128)(2,1)} %copy.11, s32[]{:T(128)} %constant.38.clone.1, s32[]{:T(128)} %constant.38.clone.1, s32[]{:T(128)} %constant.38.clone.1, s32[]{:T(128)S(6)} %select_n.51, s32[]{:T(128)} %constant.38.clone.1) | dynamic-update-slice | bytes 3932164 | tf_op jit(solution)/shard_map/dynamic_update_slice | solution.py:17
  251.6 0.0 collective-permute-done.1
  251.6 7.9 %copy.12 = bf16[8,2,15,32,128]{3,4,2,1,0:T(8,128)(2,1)} copy(bf16[8,2,15,32,128]{4,3,2,1,0:T(8,128)(2,1)} %collective-permute-done.1) | data formatting | bytes 3932160 | tf_op jit(solution)/shard_map/ppermute | solution.py:21
  259.5 98.7 %dynamic_update_slice.14 = bf16[8,2,15,128,128]{3,4,2,1,0:T(8,128)(2,1)} dynamic-update-slice(bf16[8,2,15,128,128]{3,4,2,1,0:T(8,128)(2,1)} %dynamic_update_slice.13, bf16[8,2,15,32,128]{3,4,2,1,0:T(8,128)(2,1)} %copy.12, s32[]{:T(128)} %constant.38.clone.1, s32[]{:T(128)} %constant.38.clone.1, s32[]{:T(128)} %constant.38.clone.1, s32[]{:T(128)S(6)} %select_n.53, s32[]{:T(128)} %constant.38.clone.1) | dynamic-update-slice | bytes 3932164 | tf_op jit(solution)/shard_map/dynamic_update_slice | solution.py:22
  358.2 0.0 collective-permute-done.2
  358.2 7.9 %copy.13 = bf16[8,2,15,32,128]{3,4,2,1,0:T(8,128)(2,1)} copy(bf16[8,2,15,32,128]{4,3,2,1,0:T(8,128)(2,1)} %collective-permute-done.2) | data formatting | bytes 3932160 | tf_op jit(solution)/shard_map/ppermute | solution.py:16
  366.1 98.7 %dynamic_update_slice.15 = bf16[8,2,15,128,128]{3,4,2,1,0:T(8,128)(2,1)} dynamic-update-slice(bf16[8,2,15,128,128]{3,4,2,1,0:T(8,128)(2,1)} %dynamic_update_slice.14, bf16[8,2,15,32,128]{3,4,2,1,0:T(8,128)(2,1)} %copy.13, s32[]{:T(128)} %constant.38.clone.1, s32[]{:T(128)} %constant.38.clone.1, s32[]{:T(128)} %constant.38.clone.1, s32[]{:T(128)S(6)} %select_n.55, s32[]{:T(128)} %constant.38.clone.1) | dynamic-update-slice | bytes 3932164 | tf_op jit(solution)/shard_map/dynamic_update_slice | solution.py:17
  464.9 11.5 %fusion.3 = f32[8,2,128,4,128]{4,2,3,1,0:T(8,128)} fusion(bf16[8,4,15,128,128]{4,3,2,1,0:T(8,128)(2,1)} %all-gather.2.cloned.1.call-done, bf16[8,2,15,128,128]{3,4,2,1,0:T(8,128)(2,1)} %dynamic_update_slice.15), kind=kOutput, calls=%fused_computation.3 | convolution fusion | flops 4026531840 | bytes 27787264 | tf_op jit(solution)/shard_map/gikca,gjkcb->giajb/dot_general | solution.py:25
  476.3 0.0 reduce-scatter.2.cloned.1.call-update
  476.4 0.0 copy-done
  476.4 0.1 dynamic_slice.6
  476.5 0.1 iota_compare_fusion.2
  476.5 86.4 %reduce-scatter.2.cloned.1.call-done = f32[2,2,128,4,128]{4,2,3,1,0:T(8,128)} async-done(((f32[8,2,128,4,128]{4,2,3,1,0:T(8,128)}), f32[2,2,128,4,128]{4,2,3,1,0:T(8,128)}) %reduce-scatter.2.cloned.1.call-update) | async-done | bytes 1048592 | tf_op jit(solution)/shard_map/reduce_scatter | solution.py:53
  563.0 1.3 select_convert_fusion
  564.3 1.2 copy.14
  (4 shorter events, 0.0 us)
Async XLA Ops:
  6.5 458.3 %all-gather.2.cloned.1.call-start = ((), (), s32[]{:S(2)}) async-start(), calls=%async_computation.1 | async-start | bytes 16711680 | tf_op jit(solution)/shard_map/all_gather | solution.py:28
  7.3 555.7 %reduce-scatter.2.cloned.1.call-start = ((), (), s32[]{:S(2)}) async-start(), calls=%async_computation.2 | async-start | bytes 5242880 | tf_op jit(solution)/shard_map/reduce_scatter | solution.py:53
  12.1 44.3 %collective-permute-start = (bf16[8,2,15,32,128]{4,3,2,1,0:T(8,128)(2,1)S(1)}, bf16[8,2,15,32,128]{4,3,2,1,0:T(8,128)(2,1)}, u32[]{:S(2)}, u32[]{:S(2)}) collective-permute-start(bf16[8,2,15,32,128]{4,3,2,1,0:T(8,128)(2,1)S(1)} %broadcast_select_fusion), channel_id=1, source_target_pairs={{0,4},{4,8},{8,12},{12,0},{1,5},{5,9},{9,13},{13,1},{2,6},{6,10},{... | collective-permute-start | bytes 5898248 | tf_op jit(solution)/shard_map/ppermute | solution.py:16
  14.3 237.3 %collective-permute-start.1 = (bf16[8,2,15,32,128]{4,3,2,1,0:T(8,128)(2,1)S(1)}, bf16[8,2,15,32,128]{4,3,2,1,0:T(8,128)(2,1)}, u32[]{:S(2)}, u32[]{:S(2)}) collective-permute-start(bf16[8,2,15,32,128]{4,3,2,1,0:T(8,128)(2,1)S(1)} %broadcast_select_fusion), channel_id=1, source_target_pairs={{0,12},{4,0},{8,4},{12,8},{1,13},{5,1},{9,5},{13,9},{2,14},{6,2},{... | collective-permute-start | bytes 5898248 | tf_op jit(solution)/shard_map/ppermute | solution.py:21
  56.5 301.7 %collective-permute-start.2 = (bf16[8,2,15,32,128]{4,3,2,1,0:T(8,128)(2,1)}, bf16[8,2,15,32,128]{4,3,2,1,0:T(8,128)(2,1)}, u32[]{:S(2)}, u32[]{:S(2)}) collective-permute-start(bf16[8,2,15,32,128]{4,3,2,1,0:T(8,128)(2,1)} %collective-permute-done), channel_id=1, source_target_pairs={{0,4},{4,8},{8,12},{12,0},{1,5},{5,9},{9,13},{13,1},{2,6},{6,10},{... | collective-permute-start | bytes 5898248 | tf_op jit(solution)/shard_map/ppermute | solution.py:16
  464.9 11.5 %copy-start = (s32[8]{0:T(128)S(1)}, s32[8]{0:T(128)}, u32[]{:S(2)}) copy-start(s32[8]{0:T(128)} %param.6) | copy-start | bytes 100
Sparse Core Ops, SparseCore 0:
  9.9 180.1 all-gather.1
  476.5 86.4 reduce-scatter.1
